TPU v7x, 256 devices: a whole 4x4x8 slice. The times are simulated.
256 devices in a mesh: prow: 8 (over x, core), pcol: 32 (over y, z).
Axes of the slice: x: 4, y: 4, z: 8, core: 2. Of those that a mesh axis runs over, the one named last changes fastest.
Arguments:
- factor: bfloat16 [16, 8, 4, 32, 256, 256], P(None, 'prow', None, 'pcol')
- right_side: bfloat16 [4, 32, 256, 256], P(None, 'pcol'), may hold values from -6 to 6
- node_blocks: int32 [15], replicated, may hold values from 1 to 32, as said below
- front_mask: int32 [15, 128], replicated, may hold values from 0 to 1, as said below
Outputs:
- solution: bfloat16 [4, 32, 256, 256], P(None, 'pcol')
Inputs may be any that keep to these rules, and one draw needn't show every extreme that they name: node_blocks[s] counts the blocks of node s of a complete binary elimination tree in heap order (the parent of s is (s - 1) // 2); the nodes of one depth together have 32 blocks. front_mask[s, i] is 1 only where block i belongs to a strict ancestor of node s.
All inputs are finite; a program needn't handle non-finite values.
Results may differ from a plain program's by a relative error of at most 0.024.
Values may be sent and summed in bfloat16 or wider, within the bound.
No kernel may reach another device: no remote copies, remote signals or barrier semaphores. Data moves between devices by JAX's collectives and lax.ppermute only.
A program may use at most 128 MiB of HBM per device.

v0:
```python
import jax
import jax.numpy as jnp
from jax import lax
from jax.sharding import PartitionSpec as P

LEVELS = 4


def node_order():
    ordering = []
    for depth_now in range(LEVELS - 1, -1, -1):
        ordering.extend(range(2**depth_now - 1, 2 ** (depth_now + 1) - 1))
    return ordering


def node_table(node_blocks, total_blocks):
    node_count = node_blocks.shape[0]
    ordered = jnp.array(node_order(), dtype=jnp.int32)
    node_ids = jnp.arange(node_count, dtype=jnp.int32)
    pick_sizes = (ordered[:, None] == node_ids[None, :]).astype(jnp.int32)
    level_sizes = jnp.sum(pick_sizes * node_blocks[None, :], axis=1)
    block_ends = jnp.cumsum(level_sizes)
    block_ids = jnp.arange(total_blocks, dtype=jnp.int32)
    positions = jnp.sum((block_ids[:, None] >= block_ends[None, :]).astype(jnp.int32), axis=1)
    return jnp.sum(
        (positions[:, None] == node_ids[None, :]).astype(jnp.int32) * ordered[None, :], axis=1
    )


def lookup(values_table, indices):
    positions_all = jnp.arange(values_table.shape[0], dtype=jnp.int32)
    return jnp.sum(
        (indices[:, None] == positions_all[None, :]).astype(jnp.int32) * values_table[None, :],
        axis=1,
    )


def panel_products(tile_stack, live_bits, vector):
    products = jnp.einsum("nxy,yw->nxw", tile_stack, vector, preferred_element_type=jnp.float32)
    return products * live_bits.astype(jnp.float32)[:, None, None]


def local(factor, right_side, node_blocks, front_mask):
    rows_local = factor.shape[0]
    cols_local = factor.shape[2]
    block_size = factor.shape[4]
    prow_count = lax.axis_size("prow")
    pcol_count = lax.axis_size("pcol")
    prow_index = lax.axis_index("prow")
    pcol_index = lax.axis_index("pcol")
    total_blocks = rows_local * prow_count
    level_rows = pcol_count // prow_count
    piece_rows = block_size // pcol_count
    tile_grid = factor.reshape(rows_local, cols_local, block_size, block_size)
    columns_in = right_side.reshape(cols_local, block_size, right_side.shape[3])
    block_node = node_table(node_blocks, total_blocks)
    row_ids = jnp.arange(rows_local, dtype=jnp.int32) * prow_count + prow_index
    col_ids = jnp.arange(cols_local, dtype=jnp.int32) * pcol_count + pcol_index
    row_nodes = lookup(block_node, row_ids)
    col_nodes = lookup(block_node, col_ids)
    node_ids = jnp.arange(node_blocks.shape[0], dtype=jnp.int32)
    pick_node = (col_nodes[:, None] == node_ids[None, :]).astype(jnp.int32)
    front_rows = jnp.sum(pick_node[:, :, None] * front_mask[None, :, :], axis=1)
    block_all = jnp.arange(total_blocks, dtype=jnp.int32)
    pick_row = (row_ids[:, None] == block_all[None, :]).astype(jnp.int32)
    front_bits = jnp.sum(pick_row[:, None, :] * front_rows[None, :, :], axis=2)
    diag_bits = (
        (row_nodes[:, None] == col_nodes[None, :]) & (row_ids[:, None] >= col_ids[None, :])
    ).astype(jnp.int32)

    def row_pieces(level_terms):
        rhs_width = level_terms.shape[2]
        split_rows = level_terms.reshape(level_rows, pcol_count, piece_rows, rhs_width)
        return jnp.transpose(split_rows, (1, 0, 2, 3))

    rhs_width = columns_in.shape[2]
    partial_value = jnp.zeros((rows_local, block_size, rhs_width), jnp.float32)
    solved_list = []
    for section_now in range(LEVELS):
        first_row = section_now * level_rows
        after_row = first_row + level_rows
        if section_now == 0:
            rhs_column = columns_in[0]
        else:
            mine = lax.psum_scatter(
                row_pieces(partial_value[first_row:after_row]).astype(jnp.bfloat16),
                "pcol",
                scatter_dimension=0,
                tiled=True,
            ).astype(jnp.float32)
            stacked = lax.all_gather(
                mine.reshape(level_rows, 1, piece_rows, rhs_width).astype(jnp.bfloat16),
                "prow",
                axis=1,
                tiled=True,
            ).astype(jnp.float32)
            arrived = lax.all_to_all(
                stacked.reshape(pcol_count, 1, piece_rows, rhs_width).astype(jnp.bfloat16),
                "pcol",
                split_axis=0,
                concat_axis=1,
                tiled=True,
            ).astype(jnp.float32)
            update = arrived.reshape(block_size, rhs_width)
            rhs_column = (columns_in[section_now].astype(jnp.float32) - update).astype(jnp.bfloat16)
        diag_terms = panel_products(
            tile_grid[first_row:after_row, section_now],
            diag_bits[first_row:after_row, section_now],
            rhs_column,
        )
        mine_solved = lax.psum_scatter(
            row_pieces(diag_terms).astype(jnp.bfloat16), "pcol", scatter_dimension=0, tiled=True
        )
        stacked_solved = lax.all_gather(
            mine_solved.reshape(level_rows, 1, piece_rows, rhs_width), "prow", axis=1, tiled=True
        )
        arrived_solved = lax.all_to_all(
            stacked_solved.reshape(pcol_count, 1, piece_rows, rhs_width),
            "pcol",
            split_axis=0,
            concat_axis=1,
            tiled=True,
        )
        solved = arrived_solved.reshape(block_size, rhs_width)
        solved_list.append(solved)
        if section_now + 1 < LEVELS:
            update_terms = panel_products(
                tile_grid[after_row:, section_now], front_bits[after_row:, section_now], solved
            )
            partial_value = partial_value.at[after_row:].add(update_terms)
    solution = jnp.stack(solved_list)
    return solution.reshape(cols_local, 1, block_size, columns_in.shape[2])


def solution(mesh):
    in_specs = (P(None, "prow", None, "pcol", None, None), P(None, "pcol", None, None), P(), P())
    out_specs = P(None, "pcol", None, None)
    return jax.shard_map(local, mesh=mesh, in_specs=in_specs, out_specs=out_specs, check_vma=False)
```

profile of v0, /device:TPU:2, one launch (start us, length us, event | category | flops | bytes accessed | tf_op | source)
XLA Modules:
  0.0 1263.1 jit_solution(1602754912323718388)
XLA Ops:
  6.5 0.9 select_reduce_fusion.2
  7.4 0.2 reduce-window.8
  7.7 0.7 select_reduce_fusion.1
  8.4 0.2 select_reduce_fusion.3
  9.0 7.6 copy.38
  16.6 2.2 fusion.10
  18.8 0.6 dynamic-slice.23
  19.5 149.9 %all-reduce.15.cloned.1.call-done = bf16[32,4,8,256]{3,2,0,1:T(8,128)(2,1)} async-done(((bf16[32,4,8,256]{3,2,0,1:T(8,128)(2,1)}), bf16[32,4,8,256]{3,2,0,1:T(8,128)(2,1)}) %all-reduce.15.cloned.1.call-update) | async-done | bytes 524304
  169.4 1.3 constant_dynamic-slice_fusion.6
  170.6 13.9 %all-gather = bf16[1,4,64,256]{3,2,0,1:T(8,128)(2,1)} all-gather(bf16[1,4,8,256]{3,2,0,1:T(8,128)(2,1)S(1)} %constant_dynamic-slice_fusion.6), channel_id=2, replica_groups=mesh['prow'=8,'pcol'=32] {'prow'}, dimensions={2}, use_global_device_ids=true | all-gather | bytes 147456 | tf_op jit(solution)/shard_map/all_gather | solution.py:114
  184.6 5.5 all-to-all-start
  190.4 10.5 all-to-all-done
  200.9 2.0 multiply_bitcast_fusion
  202.9 0.8 fusion.12
  203.8 142.5 %all-reduce.17.cloned.1.call-done = bf16[32,4,8,256]{3,2,0,1:T(8,128)(2,1)} async-done(((bf16[32,4,8,256]{3,2,0,1:T(8,128)(2,1)}), bf16[32,4,8,256]{3,2,0,1:T(8,128)(2,1)}) %all-reduce.17.cloned.1.call-update) | async-done | bytes 524304
  346.3 1.3 constant_dynamic-slice_fusion.5
  347.5 12.8 %all-gather.1 = bf16[1,4,64,256]{3,2,0,1:T(8,128)(2,1)S(1)} all-gather(bf16[1,4,8,256]{3,2,0,1:T(8,128)(2,1)S(1)} %constant_dynamic-slice_fusion.5), channel_id=3, replica_groups=mesh['prow'=8,'pcol'=32] {'prow'}, dimensions={2}, use_global_device_ids=true | all-gather | bytes 147456 | tf_op jit(solution)/shard_map/all_gather | solution.py:91
  360.3 16.1 %all_to_all.28 = bf16[32,1,8,256]{3,2,1,0:T(8,128)(2,1)S(1)} all-to-all(bf16[32,1,8,256]{3,2,1,0:T(8,128)(2,1)S(1)} %bitcast.191), channel_id=1, replica_groups=mesh['prow'=8,'pcol'=32] {'pcol'}, dimensions={0} | all-to-all | bytes 262144 | tf_op jit(solution)/shard_map/all_to_all | solution.py:97
  376.4 2.2 fusion.9
  378.6 142.6 %all-reduce.19.cloned.1.call-done = bf16[32,4,8,256]{3,2,0,1:T(8,128)(2,1)} async-done(((bf16[32,4,8,256]{3,2,0,1:T(8,128)(2,1)}), bf16[32,4,8,256]{3,2,0,1:T(8,128)(2,1)}) %all-reduce.19.cloned.1.call-update) | async-done | bytes 524304
  521.1 1.3 constant_dynamic-slice_fusion.4
  522.4 13.9 %all-gather.2 = bf16[1,4,64,256]{3,2,0,1:T(8,128)(2,1)} all-gather(bf16[1,4,8,256]{3,2,0,1:T(8,128)(2,1)S(1)} %constant_dynamic-slice_fusion.4), channel_id=4, replica_groups=mesh['prow'=8,'pcol'=32] {'prow'}, dimensions={2}, use_global_device_ids=true | all-gather | bytes 147456 | tf_op jit(solution)/shard_map/all_gather | solution.py:114
  536.3 5.5 all-to-all-start.2
  542.0 10.7 all-to-all-done.2
  552.6 1.7 slice_add_fusion
  554.3 1.4 copy-done
  555.7 0.8 fusion.13
  556.6 142.5 %all-reduce.21.cloned.1.call-done = bf16[32,4,8,256]{3,2,0,1:T(8,128)(2,1)} async-done(((bf16[32,4,8,256]{3,2,0,1:T(8,128)(2,1)}), bf16[32,4,8,256]{3,2,0,1:T(8,128)(2,1)}) %all-reduce.21.cloned.1.call-update) | async-done | bytes 524304
  699.1 1.3 constant_dynamic-slice_fusion.3
  700.4 12.8 %all-gather.3 = bf16[1,4,64,256]{3,2,0,1:T(8,128)(2,1)S(1)} all-gather(bf16[1,4,8,256]{3,2,0,1:T(8,128)(2,1)S(1)} %constant_dynamic-slice_fusion.3), channel_id=5, replica_groups=mesh['prow'=8,'pcol'=32] {'prow'}, dimensions={2}, use_global_device_ids=true | all-gather | bytes 147456 | tf_op jit(solution)/shard_map/all_gather | solution.py:91
  713.1 16.1 %all_to_all.29 = bf16[32,1,8,256]{3,2,1,0:T(8,128)(2,1)S(1)} all-to-all(bf16[32,1,8,256]{3,2,1,0:T(8,128)(2,1)S(1)} %bitcast.192), channel_id=1, replica_groups=mesh['prow'=8,'pcol'=32] {'pcol'}, dimensions={0} | all-to-all | bytes 262144 | tf_op jit(solution)/shard_map/all_to_all | solution.py:97
  729.2 2.2 fusion.8
  731.4 142.6 %all-reduce.23.cloned.1.call-done = bf16[32,4,8,256]{3,2,0,1:T(8,128)(2,1)} async-done(((bf16[32,4,8,256]{3,2,0,1:T(8,128)(2,1)}), bf16[32,4,8,256]{3,2,0,1:T(8,128)(2,1)}) %all-reduce.23.cloned.1.call-update) | async-done | bytes 524304
  874.0 1.3 constant_dynamic-slice_fusion.2
  875.2 13.9 %all-gather.4 = bf16[1,4,64,256]{3,2,0,1:T(8,128)(2,1)} all-gather(bf16[1,4,8,256]{3,2,0,1:T(8,128)(2,1)S(1)} %constant_dynamic-slice_fusion.2), channel_id=6, replica_groups=mesh['prow'=8,'pcol'=32] {'prow'}, dimensions={2}, use_global_device_ids=true | all-gather | bytes 147456 | tf_op jit(solution)/shard_map/all_gather | solution.py:114
  889.2 5.5 all-to-all-start.4
  894.8 10.7 all-to-all-done.4
  905.5 2.5 fusion.11
  908.0 142.4 %all-reduce.25.cloned.1.call-done = bf16[32,4,8,256]{3,2,0,1:T(8,128)(2,1)} async-done(((bf16[32,4,8,256]{3,2,0,1:T(8,128)(2,1)}), bf16[32,4,8,256]{3,2,0,1:T(8,128)(2,1)}) %all-reduce.25.cloned.1.call-update) | async-done | bytes 524304
  1050.5 1.3 constant_dynamic-slice_fusion.1
  1051.7 12.8 %all-gather.5 = bf16[1,4,64,256]{3,2,0,1:T(8,128)(2,1)S(1)} all-gather(bf16[1,4,8,256]{3,2,0,1:T(8,128)(2,1)S(1)} %constant_dynamic-slice_fusion.1), channel_id=7, replica_groups=mesh['prow'=8,'pcol'=32] {'prow'}, dimensions={2}, use_global_device_ids=true | all-gather | bytes 147456 | tf_op jit(solution)/shard_map/all_gather | solution.py:91
  1064.5 16.1 %all_to_all.30 = bf16[32,1,8,256]{3,2,1,0:T(8,128)(2,1)S(1)} all-to-all(bf16[32,1,8,256]{3,2,1,0:T(8,128)(2,1)S(1)} %bitcast.193), channel_id=1, replica_groups=mesh['prow'=8,'pcol'=32] {'pcol'}, dimensions={0} | all-to-all | bytes 262144 | tf_op jit(solution)/shard_map/all_to_all | solution.py:97
  1080.6 2.2 fusion.7
  1082.8 142.5 %all-reduce.27.cloned.1.call-done = bf16[32,4,8,256]{3,2,0,1:T(8,128)(2,1)} async-done(((bf16[32,4,8,256]{3,2,0,1:T(8,128)(2,1)}), bf16[32,4,8,256]{3,2,0,1:T(8,128)(2,1)}) %all-reduce.27.cloned.1.call-update) | async-done | bytes 524304
  1225.3 1.3 constant_dynamic-slice_fusion
  1226.5 12.8 %all-gather.6 = bf16[1,4,64,256]{3,2,0,1:T(8,128)(2,1)S(1)} all-gather(bf16[1,4,8,256]{3,2,0,1:T(8,128)(2,1)S(1)} %constant_dynamic-slice_fusion), channel_id=8, replica_groups=mesh['prow'=8,'pcol'=32] {'prow'}, dimensions={2}, use_global_device_ids=true | all-gather | bytes 147456 | tf_op jit(solution)/shard_map/all_gather | solution.py:114
  1239.3 16.1 %all_to_all.31 = bf16[32,1,8,256]{3,2,1,0:T(8,128)(2,1)S(1)} all-to-all(bf16[32,1,8,256]{3,2,1,0:T(8,128)(2,1)S(1)} %bitcast.194), channel_id=1, replica_groups=mesh['prow'=8,'pcol'=32] {'pcol'}, dimensions={0} | all-to-all | bytes 262144 | tf_op jit(solution)/shard_map/all_to_all | solution.py:117
  1255.4 0.9 maximum_bitcast_fusion
  (32 shorter events, 1.3 us)
Async XLA Ops:
  6.5 162.9 %all-reduce.15.cloned.1.call-start = ((), (), s32[]{:S(2)}) async-start(), calls=%async_computation.7 | async-start | bytes 1048576
  8.9 9.8 copy-start.2
  8.9 10.4 copy-start.1
  184.6 16.3 %all-to-all-start = ((bf16[32,1,8,256]{3,2,1,0:T(8,128)(2,1)}), bf16[32,1,8,256]{3,2,1,0:T(8,128)(2,1)S(1)}, u32[]{:S(2)}, u32[]{:S(2)}) async-start(bf16[32,1,8,256]{3,2,1,0:T(8,128)(2,1)} %bitcast.10), calls=%async_computation | async-start | bytes 262144 | tf_op jit(solution)/shard_map/all_to_all | solution.py:117
  190.1 156.2 %all-reduce.17.cloned.1.call-start = ((), (), s32[]{:S(2)}) async-start(), calls=%async_computation.8 | async-start | bytes 1048576
  203.7 317.4 %all-reduce.19.cloned.1.call-start = ((), (), s32[]{:S(2)}) async-start(), calls=%async_computation.9 | async-start | bytes 1048576
  536.3 16.3 %all-to-all-start.2 = ((bf16[32,1,8,256]{3,2,1,0:T(8,128)(2,1)}), bf16[32,1,8,256]{3,2,1,0:T(8,128)(2,1)S(1)}, u32[]{:S(2)}, u32[]{:S(2)}) async-start(bf16[32,1,8,256]{3,2,1,0:T(8,128)(2,1)} %bitcast.30), calls=%async_computation.2 | async-start | bytes 262144 | tf_op jit(solution)/shard_map/all_to_all | solution.py:117
  541.8 157.2 %all-reduce.21.cloned.1.call-start = ((), (), s32[]{:S(2)}) async-start(), calls=%async_computation.10 | async-start | bytes 1048576
  554.3 1.4 copy-start
  556.6 317.4 %all-reduce.23.cloned.1.call-start = ((), (), s32[]{:S(2)}) async-start(), calls=%async_computation.11 | async-start | bytes 1048576
  889.2 16.3 %all-to-all-start.4 = ((bf16[32,1,8,256]{3,2,1,0:T(8,128)(2,1)}), bf16[32,1,8,256]{3,2,1,0:T(8,128)(2,1)S(1)}, u32[]{:S(2)}, u32[]{:S(2)}) async-start(bf16[32,1,8,256]{3,2,1,0:T(8,128)(2,1)} %bitcast.50), calls=%async_computation.4 | async-start | bytes 262144 | tf_op jit(solution)/shard_map/all_to_all | solution.py:117
  894.7 155.8 %all-reduce.25.cloned.1.call-start = ((), (), s32[]{:S(2)}) async-start(), calls=%async_computation.12 | async-start | bytes 1048576
  908.0 317.3 %all-reduce.27.cloned.1.call-start = ((), (), s32[]{:S(2)}) async-start(), calls=%async_computation.13 | async-start | bytes 1048576
Sparse Core Ops, SparseCore 0:
  18.9 150.4 all-reduce.14
  203.9 142.3 all-reduce.16
  378.7 142.3 all-reduce.18
  556.7 142.3 all-reduce.20
  731.5 142.3 all-reduce.22
  908.1 142.3 all-reduce.24
  1082.9 142.2 all-reduce.26
where the time goes:
time: 1260 us
  waiting for transfers between devices  1040 us (83%)
  blocking collectives  157 us (12%)
  local copies, waits for them, and re-layouts  20.1 us (2%)
  starting transfers between devices  16.8 us (1%)
  matrix products  14.9 us (1%)
  between operations  13.6 us (1%)
    unnamed x14, waiting for transfers between devices  1000 us
    all_gather x4, blocking collectives, local(): lax.all_gather(mine_solved.reshape(level_rows, 1, piece_rows, rhs_width),...  54.5 us
    all_to_all x3, blocking collectives, local(): lax.all_to_all(stacked.reshape(pcol_count, 1, piece_rows, rhs_width).asty...  48.2 us
    all_gather x3, blocking collectives, local(): lax.all_gather(mine.reshape(level_rows, 1, piece_rows, rhs_width).astype(...  38.3 us
    all_to_all x3, waiting for transfers between devices, local(): lax.all_to_all(stacked_solved.reshape(pcol_count, 1, piece_rows, rhs_widt...  31.9 us
  transfers between devices with their start and end apart: 10, of which 10 were waited for; matrix products, arithmetic and copies ran while one was open for 0% of the time, Pallas kernels for 0%

commit v1 on v0

--- a/solution.py
+++ b/solution.py
@@ -114,12 +114,20 @@
         stacked_solved = lax.all_gather(
             mine_solved.reshape(level_rows, 1, piece_rows, rhs_width), "prow", axis=1, tiled=True
         )
-        arrived_solved = lax.all_to_all(
-            stacked_solved.reshape(pcol_count, 1, piece_rows, rhs_width),
-            "pcol",
-            split_axis=0,
-            concat_axis=1,
-            tiled=True,
+        arrived_solved = jnp.concatenate(
+            lax.all_to_all(
+                jnp.stack(
+                    jnp.split(
+                        stacked_solved.reshape(pcol_count, 1, piece_rows, rhs_width),
+                        lax.axis_size("pcol"),
+                        axis=0,
+                    )
+                ),
+                "pcol",
+                0,
+                0,
+            ),
+            axis=1,
         )
         solved = arrived_solved.reshape(block_size, rhs_width)
         solved_list.append(solved)

time: 1260 us -> 1320 us (1.048)
  local copies, waits for them, and re-layouts: 20.1 us -> 77.1 us
    unnamed x15 -> x139, local copies, waits for them, and re-layouts: 18.4 us -> 73.7 us
where the time goes in v1:
time: 1320 us
  waiting for transfers between devices  1040 us (79%)
  blocking collectives  154 us (12%)
  local copies, waits for them, and re-layouts  77.1 us (6%)
  starting transfers between devices  16.7 us (1%)
  matrix products  14.9 us (1%)
  between operations  13.8 us (1%)
    unnamed x14, waiting for transfers between devices  1000 us
    unnamed x139, local copies, waits for them, and re-layouts  73.7 us
    all_gather x4, blocking collectives, local(): lax.all_gather(mine_solved.reshape(level_rows, 1, piece_rows, rhs_width),...  51 us
    all_to_all x3, blocking collectives, local(): lax.all_to_all(stacked.reshape(pcol_count, 1, piece_rows, rhs_width).asty...  48.2 us
    all_gather x3, blocking collectives, local(): lax.all_gather(mine.reshape(level_rows, 1, piece_rows, rhs_width).astype(...  38.3 us
    all_to_all x3, waiting for transfers between devices, local(): lax.all_to_all(jnp.stack(jnp.split(stacked_solved.reshape(pcol_count, 1,...  31.9 us
  transfers between devices with their start and end apart: 10, of which 10 were waited for; matrix products, arithmetic and copies ran while one was open for 0% of the time, Pallas kernels for 0%

profile of v1, /device:TPU:2, one launch (start us, length us, event | category | flops | bytes accessed | tf_op | source)
XLA Modules:
  0.0 1316.9 jit_solution(14167822594698813205)
XLA Ops:
  6.5 0.9 select_reduce_fusion.2
  7.7 0.7 select_reduce_fusion.1
  9.0 7.6 copy.414
  16.6 2.2 fusion.10
  19.5 149.9 %all-reduce.15.cloned.1.call-done = bf16[32,4,8,256]{3,2,0,1:T(8,128)(2,1)} async-done(((bf16[32,4,8,256]{3,2,0,1:T(8,128)(2,1)}), bf16[32,4,8,256]{3,2,0,1:T(8,128)(2,1)}) %all-reduce.15.cloned.1.call-update) | async-done | bytes 524304
  169.4 1.3 constant_dynamic-slice_fusion.6
  170.6 12.8 all-gather
  183.4 0.6 constant_dynamic-update-slice_fusion.31
  184.0 0.6 constant_dynamic-update-slice_fusion.30
  184.6 0.6 constant_dynamic-update-slice_fusion.29
  202.4 5.5 all-to-all-start
  208.2 10.5 all-to-all-done
  218.7 2.0 multiply_bitcast_fusion
  220.7 0.8 fusion.12
  221.6 142.5 %all-reduce.17.cloned.1.call-done = bf16[32,4,8,256]{3,2,0,1:T(8,128)(2,1)} async-done(((bf16[32,4,8,256]{3,2,0,1:T(8,128)(2,1)}), bf16[32,4,8,256]{3,2,0,1:T(8,128)(2,1)}) %all-reduce.17.cloned.1.call-update) | async-done | bytes 524304
  364.1 1.3 constant_dynamic-slice_fusion.5
  365.3 12.8 all-gather.1
  378.1 16.1 %all_to_all.47 = bf16[32,1,8,256]{3,2,1,0:T(8,128)(2,1)S(1)} all-to-all(bf16[32,1,8,256]{3,2,1,0:T(8,128)(2,1)S(1)} %bitcast.955), channel_id=1, replica_groups=mesh['prow'=8,'pcol'=32] {'pcol'}, dimensions={0} | all-to-all | bytes 262144 | tf_op jit(solution)/shard_map/all_to_all | solution.py:97
  394.2 2.2 fusion.9
  396.4 142.5 %all-reduce.19.cloned.1.call-done = bf16[32,4,8,256]{3,2,0,1:T(8,128)(2,1)} async-done(((bf16[32,4,8,256]{3,2,0,1:T(8,128)(2,1)}), bf16[32,4,8,256]{3,2,0,1:T(8,128)(2,1)}) %all-reduce.19.cloned.1.call-update) | async-done | bytes 524304
  538.9 1.3 constant_dynamic-slice_fusion.4
  540.2 12.8 all-gather.2
  571.9 5.5 all-to-all-start.2
  577.6 10.7 all-to-all-done.2
  588.2 1.7 slice_add_fusion
  589.9 1.4 copy-done
  591.3 0.8 fusion.13
  592.2 142.5 %all-reduce.21.cloned.1.call-done = bf16[32,4,8,256]{3,2,0,1:T(8,128)(2,1)} async-done(((bf16[32,4,8,256]{3,2,0,1:T(8,128)(2,1)}), bf16[32,4,8,256]{3,2,0,1:T(8,128)(2,1)}) %all-reduce.21.cloned.1.call-update) | async-done | bytes 524304
  734.7 1.3 constant_dynamic-slice_fusion.3
  736.0 12.8 all-gather.3
  748.7 16.1 %all_to_all.48 = bf16[32,1,8,256]{3,2,1,0:T(8,128)(2,1)S(1)} all-to-all(bf16[32,1,8,256]{3,2,1,0:T(8,128)(2,1)S(1)} %bitcast.956), channel_id=1, replica_groups=mesh['prow'=8,'pcol'=32] {'pcol'}, dimensions={0} | all-to-all | bytes 262144 | tf_op jit(solution)/shard_map/all_to_all | solution.py:97
  764.8 2.2 fusion.8
  767.0 142.5 %all-reduce.23.cloned.1.call-done = bf16[32,4,8,256]{3,2,0,1:T(8,128)(2,1)} async-done(((bf16[32,4,8,256]{3,2,0,1:T(8,128)(2,1)}), bf16[32,4,8,256]{3,2,0,1:T(8,128)(2,1)}) %all-reduce.23.cloned.1.call-update) | async-done | bytes 524304
  909.6 1.3 constant_dynamic-slice_fusion.2
  910.8 12.8 all-gather.4
  942.6 5.5 all-to-all-start.4
  948.2 10.7 all-to-all-done.4
  958.9 2.5 fusion.11
  961.4 142.5 %all-reduce.25.cloned.1.call-done = bf16[32,4,8,256]{3,2,0,1:T(8,128)(2,1)} async-done(((bf16[32,4,8,256]{3,2,0,1:T(8,128)(2,1)}), bf16[32,4,8,256]{3,2,0,1:T(8,128)(2,1)}) %all-reduce.25.cloned.1.call-update) | async-done | bytes 524304
  1103.9 1.3 constant_dynamic-slice_fusion.1
  1105.2 12.8 all-gather.5
  1117.9 16.1 %all_to_all.49 = bf16[32,1,8,256]{3,2,1,0:T(8,128)(2,1)S(1)} all-to-all(bf16[32,1,8,256]{3,2,1,0:T(8,128)(2,1)S(1)} %bitcast.957), channel_id=1, replica_groups=mesh['prow'=8,'pcol'=32] {'pcol'}, dimensions={0} | all-to-all | bytes 262144 | tf_op jit(solution)/shard_map/all_to_all | solution.py:97
  1134.0 2.2 fusion.7
  1136.3 142.5 %all-reduce.27.cloned.1.call-done = bf16[32,4,8,256]{3,2,0,1:T(8,128)(2,1)} async-done(((bf16[32,4,8,256]{3,2,0,1:T(8,128)(2,1)}), bf16[32,4,8,256]{3,2,0,1:T(8,128)(2,1)}) %all-reduce.27.cloned.1.call-update) | async-done | bytes 524304
  1278.8 1.3 constant_dynamic-slice_fusion
  1280.0 12.8 all-gather.6
  1293.1 16.1 %all_to_all.50 = bf16[32,1,1,8,256]{4,3,2,1,0:T(8,128)(2,1)S(1)} all-to-all(bf16[32,1,1,8,256]{4,3,2,1,0:T(8,128)(2,1)S(1)} %constant_dynamic-update-slice_fusion.96), channel_id=1, replica_groups=mesh['prow'=8,'pcol'=32] {'pcol'}, dimensions={0} | all-to-all | bytes 262144 | tf_op jit(solution)/shard_map/all_to_all | solution.py:118
  1309.2 0.9 maximum_bitcast_fusion
  (160 shorter events, 57.5 us)
Async XLA Ops:
  6.5 162.9 %all-reduce.15.cloned.1.call-start = ((), (), s32[]{:S(2)}) async-start(), calls=%async_computation.7 | async-start | bytes 1048576
  8.9 9.8 copy-start.2
  8.9 10.4 copy-start.1
  202.4 16.3 %all-to-all-start = ((bf16[32,1,1,8,256]{4,3,2,1,0:T(8,128)(2,1)}), bf16[32,1,1,8,256]{4,3,2,1,0:T(8,128)(2,1)S(1)}, u32[]{:S(2)}, u32[]{:S(2)}) async-start(bf16[32,1,1,8,256]{4,3,2,1,0:T(8,128)(2,1)} %constant_dynamic-update-slice_fusion), calls=%async_computation | async-start | bytes 262144 | tf_op jit(solution)/shard_map/all_to_all | solution.py:118
  207.9 156.2 %all-reduce.17.cloned.1.call-start = ((), (), s32[]{:S(2)}) async-start(), calls=%async_computation.8 | async-start | bytes 1048576
  221.6 317.4 %all-reduce.19.cloned.1.call-start = ((), (), s32[]{:S(2)}) async-start(), calls=%async_computation.9 | async-start | bytes 1048576
  571.9 16.3 %all-to-all-start.2 = ((bf16[32,1,1,8,256]{4,3,2,1,0:T(8,128)(2,1)}), bf16[32,1,1,8,256]{4,3,2,1,0:T(8,128)(2,1)S(1)}, u32[]{:S(2)}, u32[]{:S(2)}) async-start(bf16[32,1,1,8,256]{4,3,2,1,0:T(8,128)(2,1)} %constant_dynamic-update-slice_fusion.32), calls=%async_computation.2 | async-start | bytes 262144 | tf_op jit(solution)/shard_map/all_to_all | solution.py:118
  577.4 157.3 %all-reduce.21.cloned.1.call-start = ((), (), s32[]{:S(2)}) async-start(), calls=%async_computation.10 | async-start | bytes 1048576
  589.9 1.4 copy-start
  592.2 317.4 %all-reduce.23.cloned.1.call-start = ((), (), s32[]{:S(2)}) async-start(), calls=%async_computation.11 | async-start | bytes 1048576
  942.6 16.3 %all-to-all-start.4 = ((bf16[32,1,1,8,256]{4,3,2,1,0:T(8,128)(2,1)}), bf16[32,1,1,8,256]{4,3,2,1,0:T(8,128)(2,1)S(1)}, u32[]{:S(2)}, u32[]{:S(2)}) async-start(bf16[32,1,1,8,256]{4,3,2,1,0:T(8,128)(2,1)} %constant_dynamic-update-slice_fusion.64), calls=%async_computation.4 | async-start | bytes 262144 | tf_op jit(solution)/shard_map/all_to_all | solution.py:118
  948.1 155.8 %all-reduce.25.cloned.1.call-start = ((), (), s32[]{:S(2)}) async-start(), calls=%async_computation.12 | async-start | bytes 1048576
  961.4 317.4 %all-reduce.27.cloned.1.call-start = ((), (), s32[]{:S(2)}) async-start(), calls=%async_computation.13 | async-start | bytes 1048576
Sparse Core Ops, SparseCore 0:
  18.9 150.4 all-reduce.14
  221.7 142.3 all-reduce.16
  396.5 142.3 all-reduce.18
  592.3 142.3 all-reduce.20
  767.2 142.3 all-reduce.22
  961.5 142.3 all-reduce.24
  1136.4 142.3 all-reduce.26
